TPU v7x, 256 devices: a whole 4x4x8 slice. The times are simulated.
256 devices in a mesh: row: 32 (over y, x, core), col: 8 (over z).
Axes of the slice: x: 4, y: 4, z: 8, core: 2. Of those that a mesh axis runs over, the one named last changes fastest.
Arguments:
- start_block: float32 [8192, 256], P(('col', 'row')), may hold values from -6 to 6
- tile_values: float32 [32, 8, 2, 256, 256], P('row', 'col'), may hold values from -0.0625 to 0.0625
- tile_rows: int32 [32, 8, 2], P('row', 'col'), may hold values from 0 to 0, as said below
- tile_cols: int32 [32, 8, 2], P('row', 'col'), may hold values from 0 to 3
- tile_count: int32 [32, 8], P('row', 'col'), may hold values from 1 to 2, as said below
Outputs:
- image_block: float32 [8192, 256], P('row')
- new_basis: float32 [8192, 256], P(('col', 'row'))
- factor: float32 [256, 256], replicated
Inputs may be any that keep to these rules, and one draw needn't show every extreme that they name: On each device the slots name distinct positions (tile_rows, tile_cols) of its 1 x 4 grid of blocks, slots at or beyond tile_count included. `tile_count`: some devices hold exactly 2 live tiles.
All inputs are finite; a program needn't handle non-finite values.
Results may differ from a plain program's by a relative error of at most 0.0001.
Values sent between devices are 32-bit elements; how exact they have to be, the bound alone decides.
No kernel may reach another device: no remote copies, remote signals or barrier semaphores. Data moves between devices by JAX's collectives and lax.ppermute only.
A program may use at most 64 MiB of HBM per device.

v0:
```python
import jax
import jax.numpy as jnp
from jax import lax
from jax.sharding import PartitionSpec as P

BR = 1


def cholesky_lower(gram):
    size = gram.shape[0]
    index = jnp.arange(size, dtype=jnp.int32)

    def column_step(j, lower):
        known = lower * (index[None, :] < j).astype(gram.dtype)
        row_j = lax.dynamic_slice_in_dim(known, j, 1, 0)[0]
        column = lax.dynamic_slice_in_dim(gram, j, 1, 1)[:, 0] - jnp.dot(
            known, row_j, precision=lax.Precision.HIGHEST
        )
        pivot = jnp.sqrt(lax.dynamic_slice_in_dim(column, j, 1, 0)[0])
        column = jnp.where(index >= j, column / pivot, jnp.zeros_like(column))
        return lax.dynamic_update_slice_in_dim(lower, column[:, None], j, 1)

    return lax.fori_loop(0, size, column_step, jnp.zeros_like(gram))


def lower_inverse(lower):
    size = lower.shape[0]
    index = jnp.arange(size, dtype=jnp.int32)

    def row_step(i, inverse):
        row_l = lax.dynamic_slice_in_dim(lower, i, 1, 0)[0]
        known = row_l * (index < i).astype(lower.dtype)
        unit = (index == i).astype(lower.dtype)
        pivot = lax.dynamic_slice_in_dim(row_l, i, 1, 0)[0]
        new_row = (unit - jnp.dot(known, inverse, precision=lax.Precision.HIGHEST)) / pivot
        return lax.dynamic_update_slice_in_dim(inverse, new_row[None, :], i, 0)

    return lax.fori_loop(0, size, row_step, jnp.zeros_like(lower))


def body(start_block, tile_values, tile_rows, tile_cols, tile_count):
    tile_size = tile_values.shape[-1]
    basis_width = start_block.shape[1]
    slot_total = tile_values.shape[2]
    slab = lax.all_gather(start_block, "row", axis=0, tiled=True)
    start_blocks = slab.reshape(-1, tile_size, basis_width)
    block_cols = start_blocks.shape[0]
    values = tile_values.reshape(slot_total, tile_size, tile_size)
    row_ids = tile_rows.reshape(slot_total)
    col_ids = tile_cols.reshape(slot_total)
    live_count = tile_count.reshape(())
    block_rows = BR
    live_mask = (jnp.arange(slot_total, dtype=jnp.int32) < live_count).astype(jnp.float32)
    row_onehot = (row_ids[:, None] == jnp.arange(block_rows, dtype=jnp.int32)[None, :]).astype(
        jnp.float32
    ) * live_mask[:, None]
    products = jnp.einsum(
        "tij,tjk->tik",
        values,
        start_blocks[col_ids],
        precision=lax.Precision.HIGHEST,
        preferred_element_type=jnp.float32,
    )
    partial_image = jnp.einsum(
        "tb,tik->bik",
        row_onehot,
        products,
        precision=lax.Precision.HIGHEST,
        preferred_element_type=jnp.float32,
    )
    partial_rows = partial_image.reshape(-1, basis_width)
    image_block = lax.psum(partial_rows, "col")
    image_blocks = image_block.reshape(block_rows, tile_size, basis_width)
    col_onehot = (col_ids[:, None] == jnp.arange(block_cols, dtype=jnp.int32)[None, :]).astype(
        jnp.float32
    ) * live_mask[:, None]
    back_products = jnp.einsum(
        "tji,tjk->tik",
        values,
        image_blocks[row_ids],
        precision=lax.Precision.HIGHEST,
        preferred_element_type=jnp.float32,
    )
    partial_projected = jnp.einsum(
        "tc,tik->cik",
        col_onehot,
        back_products,
        precision=lax.Precision.HIGHEST,
        preferred_element_type=jnp.float32,
    )
    partial_flat = partial_projected.reshape(-1, basis_width)
    projected = lax.psum_scatter(partial_flat, "row", scatter_dimension=0, tiled=True)
    share_rows = projected.shape[0]
    matrix_order = share_rows * lax.axis_size("row") * lax.axis_size("col")
    local_gram = jnp.dot(
        projected.T, projected, precision=lax.Precision.HIGHEST, preferred_element_type=jnp.float32
    )
    gram_matrix = lax.psum(local_gram, ("row", "col")) / matrix_order
    lower = cholesky_lower(gram_matrix)
    inverse = lower_inverse(lower)
    factor = lower.T
    new_basis = jnp.dot(
        projected, inverse.T, precision=lax.Precision.HIGHEST, preferred_element_type=jnp.float32
    )
    return (image_block, new_basis, factor)


def solution(mesh):
    placed = (
        P(("col", "row"), None),
        P("row", "col", None, None, None),
        P("row", "col", None),
        P("row", "col", None),
        P("row", "col"),
    )
    return jax.shard_map(
        body,
        mesh=mesh,
        in_specs=placed,
        out_specs=(P("row", None), P(("col", "row"), None), P()),
        check_vma=False,
    )
```

profile of v0, /device:TPU:2, one launch (start us, length us, event | category | flops | bytes accessed | tf_op | source)
XLA Modules:
  0.0 1525.9 jit_solution(4812023314239359038)
XLA Ops:
  7.2 0.7 all-gather.2.cloned.1.call-update
  8.7 52.4 %all-gather.2.cloned.1.call-done = f32[1024,256]{1,0:T(8,128)} async-done(((f32[32,256]{1,0:T(8,128)}), f32[1024,256]{1,0:T(8,128)}) %all-gather.2.cloned.1.call-update) | async-done | bytes 1048592 | tf_op jit(solution)/shard_map/all_gather | solution.py:45
  61.0 1.8 gather_fusion
  62.8 1.0 convolution_bitcast_fusion.1
  64.8 1.8 fusion.22
  66.6 0.7 copy.30
  67.4 72.3 %all-reduce.3.cloned.1.call-done = f32[256,256]{1,0:T(8,128)} async-done(((f32[256,256]{1,0:T(8,128)}), f32[256,256]{1,0:T(8,128)}) %all-reduce.3.cloned.1.call-update) | async-done | bytes 262160 | tf_op jit(solution)/shard_map/psum | solution.py:72
  139.7 1.1 copy.21
  141.6 2.3 fusion.14
  143.9 1.2 copy.23
  145.2 83.4 %reduce-scatter.2.cloned.1.call-done = f32[32,256]{1,0:T(8,128)} async-done(((f32[1024,256]{1,0:T(8,128)}), f32[32,256]{1,0:T(8,128)}) %reduce-scatter.2.cloned.1.call-update) | async-done | bytes 32784 | tf_op jit(solution)/shard_map/reduce_scatter | solution.py:92
  228.5 2.0 fusion.30
  230.5 254.0 %all-reduce.5.cloned.1.call-done = f32[256,256]{1,0:T(8,128)} async-done(((f32[256,256]{1,0:T(8,128)}), f32[256,256]{1,0:T(8,128)}) %all-reduce.5.cloned.1.call-update) | async-done | bytes 262160 | tf_op jit(solution)/shard_map/psum | solution.py:98
  484.5 1.0 broadcast_multiply_fusion.1
  485.6 631.3 %while.33 = (s32[]{:T(128)}, f32[256,256]{1,0:T(8,128)S(1)}, f32[256,256]{0,1:T(8,128)S(1)}, s32[]{:T(128)}, s32[]{:T(128)}) while((s32[]{:T(128)}, f32[256,256]{1,0:T(8,128)S(1)}, f32[256,256]{0,1:T(8,128)S(1)}, s32[]{:T(128)}, s32[]{:T(128)}) %tuple.82), condition=%wide.region_4.5_spmd.clone.clone, body=%wide.region_3.4_spmd.clone.clone.sunk | while | flops 853506 | bytes 801897 | solution.py:23
  1116.9 0.8 copy.25
  1117.8 399.9 %while.34 = (s32[]{:T(128)}, f32[256,256]{1,0:T(8,128)S(1)}, f32[256,256]{1,0:T(8,128)S(1)}, s32[]{:T(128)}, s32[]{:T(128)}, /*index=5*/s32[]{:T(128)}) while((s32[]{:T(128)}, f32[256,256]{1,0:T(8,128)S(1)}, f32[256,256]{1,0:T(8,128)S(1)}, s32[]{:T(128)}, s32[]{:T(128)}, /*index=5*/s32[]{:T(128)}) %tuple.85), condition=%wide.region_6.7_spmd.clone.clone, body=%wide.region_5.6_spmd.clone.clone.sunk | while | flops 787971 | bytes 272501 | solution.py:38
  1123.3 0.6 fusion.55
  1129.6 0.6 fusion.55
  1134.2 0.6 fusion.55
  1135.8 0.6 fusion.55
  1140.5 0.6 fusion.55
  1142.1 0.6 fusion.55
  1146.7 0.6 fusion.55
  1153.0 0.6 fusion.55
  1159.2 0.6 fusion.55
  1163.9 0.6 fusion.55
  1165.5 0.6 fusion.55
  1170.2 0.6 fusion.55
  1171.7 0.6 fusion.55
  1176.4 0.6 fusion.55
  1182.7 0.6 fusion.55
  1188.9 0.6 fusion.55
  1193.6 0.6 fusion.55
  1195.2 0.6 fusion.55
  1199.9 0.6 fusion.55
  1201.4 0.6 fusion.55
  1206.1 0.6 fusion.55
  1212.4 0.6 fusion.55
  1218.6 0.6 fusion.55
  1223.3 0.6 fusion.55
  1224.9 0.6 fusion.55
  1229.5 0.6 fusion.55
  1231.1 0.6 fusion.55
  1235.8 0.6 fusion.55
  1242.0 0.6 fusion.55
  1517.7 1.0 fusion.31
  1518.7 0.7 copy.50
  (3837 shorter events, 808.1 us)
Async XLA Ops:
  7.2 55.7 %copy-start = (f32[1,1,2,256,256]{4,3,2,1,0:T(8,128)S(1)}, f32[1,1,2,256,256]{4,3,2,1,0:T(8,128)}, u32[]{:S(2)}) copy-start(f32[1,1,2,256,256]{4,3,2,1,0:T(8,128)} %param.10) | copy-start | bytes 1572868
  7.2 53.8 %all-gather.2.cloned.1.call-start = ((), (), s32[]{:S(2)}) async-start(), calls=%async_computation.1 | async-start | bytes 1081344 | tf_op jit(solution)/shard_map/all_gather | solution.py:45
  7.9 0.7 copy-start.3
  7.9 131.7 %all-reduce.3.cloned.1.call-start = ((), (), s32[]{:S(2)}) async-start(), calls=%async_computation.2 | async-start | bytes 524288 | tf_op jit(solution)/shard_map/psum | solution.py:72
  64.1 0.7 copy-start.4
  67.4 161.2 %reduce-scatter.2.cloned.1.call-start = ((), (), s32[]{:S(2)}) async-start(), calls=%async_computation.3 | async-start | bytes 1081344 | tf_op jit(solution)/shard_map/reduce_scatter | solution.py:92
  145.1 339.4 %all-reduce.5.cloned.1.call-start = ((), (), s32[]{:S(2)}) async-start(), calls=%async_computation.4 | async-start | bytes 524288 | tf_op jit(solution)/shard_map/psum | solution.py:98
  1117.8 399.9 %copy-start.2 = (f32[32,256]{1,0:T(8,128)S(1)}, f32[32,256]{1,0:T(8,128)}, u32[]{:S(2)}) copy-start(f32[32,256]{1,0:T(8,128)} %reduce-scatter.2.cloned.1.call-done) | copy-start | bytes 98308
  1517.7 1.0 copy-start.1
Sparse Core Ops, SparseCore 0:
  10.6 50.4 all-gather.1
  67.5 72.1 all-reduce.2
  145.3 83.2 reduce-scatter.1
  234.4 250.0 all-reduce.4
where the time goes:
time: 1530 us
  local copies, waits for them, and re-layouts  539 us (35%)
  waiting for transfers between devices  463 us (30%)
  loops' own time  206 us (13%)
  other arithmetic  177 us (12%)
  matrix products  126 us (8%)
    psum x1, waiting for transfers between devices, body(): gram_matrix = lax.psum(local_gram, ('row', 'col')) / matrix_order  254 us
    another operation x1, loops' own time, cholesky_lower(): return lax.fori_loop(0, size, column_step, jnp.zeros_like(gram))  195 us
    div x256, other arithmetic, row_step(): (unit - jnp.dot(known, inverse, precision=lax.Precision.HIGHEST)) / pivot  166 us
    dynamic_slice x256, local copies, waits for them, and re-layouts, row_step(): pivot = lax.dynamic_slice_in_dim(row_l, i, 1, 0)[0]  161 us
    dynamic_update_slice x256, local copies, waits for them, and re-layouts, column_step(): return lax.dynamic_update_slice_in_dim(lower, column[:, None], j, 1)  157 us
    dynamic_slice x256, local copies, waits for them, and re-layouts, column_step(): pivot = jnp.sqrt(lax.dynamic_slice_in_dim(column, j, 1, 0)[0])  151 us
    reduce_scatter x1, waiting for transfers between devices, body(): lax.psum_scatter(partial_flat, 'row', scatter_dimension=0, tiled=True)  83.4 us
    psum x1, waiting for transfers between devices, body(): image_block = lax.psum(partial_rows, 'col')  72.3 us
  transfers between devices with their start and end apart: 4, of which 4 were waited for; matrix products, arithmetic and copies ran while one was open for 0% of the time, Pallas kernels for 0%

commit v1 on v0

--- a/solution.py
+++ b/solution.py
@@ -42,7 +42,9 @@
     tile_size = tile_values.shape[-1]
     basis_width = start_block.shape[1]
     slot_total = tile_values.shape[2]
-    slab = lax.all_gather(start_block, "row", axis=0, tiled=True)
+    slab = jnp.concatenate(
+        lax.all_to_all(jnp.stack([start_block] * lax.axis_size("row")), "row", 0, 0), axis=0
+    )
     start_blocks = slab.reshape(-1, tile_size, basis_width)
     block_cols = start_blocks.shape[0]
     values = tile_values.reshape(slot_total, tile_size, tile_size)

time: 1530 us -> 1500 us (0.980)
  waiting for transfers between devices: 463 us -> 426 us
    all_gather x1 -> x0, waiting for transfers between devices: 52.4 us -> none  [body(): slab = lax.all_gather(start_block, 'row', axis=0, tiled=True)]
    all_to_all x0 -> x1, waiting for transfers between devices: none -> 15.4 us  [body(): lax.all_to_all(jnp.stack([start_block] * lax.axis_size('row')), 'row', 0, 0)]
where the time goes in v1:
time: 1500 us
  local copies, waits for them, and re-layouts  540 us (36%)
  waiting for transfers between devices  426 us (28%)
  loops' own time  206 us (14%)
  other arithmetic  177 us (12%)
  matrix products  126 us (8%)
    psum x1, waiting for transfers between devices, body(): gram_matrix = lax.psum(local_gram, ('row', 'col')) / matrix_order  254 us
    another operation x1, loops' own time, cholesky_lower(): return lax.fori_loop(0, size, column_step, jnp.zeros_like(gram))  195 us
    div x256, other arithmetic, row_step(): (unit - jnp.dot(known, inverse, precision=lax.Precision.HIGHEST)) / pivot  166 us
    dynamic_slice x256, local copies, waits for them, and re-layouts, row_step(): pivot = lax.dynamic_slice_in_dim(row_l, i, 1, 0)[0]  161 us
    dynamic_update_slice x256, local copies, waits for them, and re-layouts, column_step(): return lax.dynamic_update_slice_in_dim(lower, column[:, None], j, 1)  157 us
    dynamic_slice x256, local copies, waits for them, and re-layouts, column_step(): pivot = jnp.sqrt(lax.dynamic_slice_in_dim(column, j, 1, 0)[0])  151 us
    reduce_scatter x1, waiting for transfers between devices, body(): lax.psum_scatter(partial_flat, 'row', scatter_dimension=0, tiled=True)  83.4 us
    psum x1, waiting for transfers between devices, body(): image_block = lax.psum(partial_rows, 'col')  72.7 us
  transfers between devices with their start and end apart: 4, of which 4 were waited for; matrix products, arithmetic and copies ran while one was open for 0% of the time, Pallas kernels for 0%

profile of v1, /device:TPU:2, one launch (start us, length us, event | category | flops | bytes accessed | tf_op | source)
XLA Modules:
  0.0 1497.0 jit_solution(10159560361448486694)
XLA Ops:
  7.2 1.9 stack.2
  9.1 7.6 all-to-all-start
  17.4 15.4 %all-to-all-done = f32[32,32,256]{2,1,0:T(8,128)S(1)} async-done(((f32[32,32,256]{2,1,0:T(8,128)}), f32[32,32,256]{2,1,0:T(8,128)S(1)}, u32[]{:S(2)}, u32[]{:S(2)}) %all-to-all-start) | async-done | bytes 1048608 | tf_op jit(solution)/shard_map/all_to_all | solution.py:46
  33.4 1.0 convolution_bitcast_fusion.1
  35.4 1.8 fusion.22
  37.2 0.7 copy.30
  38.0 72.7 %all-reduce.3.cloned.1.call-done = f32[256,256]{1,0:T(8,128)} async-done(((f32[256,256]{1,0:T(8,128)}), f32[256,256]{1,0:T(8,128)}) %all-reduce.3.cloned.1.call-update) | async-done | bytes 262160 | tf_op jit(solution)/shard_map/psum | solution.py:74
  110.7 1.1 copy.21
  112.6 2.3 fusion.14
  114.9 1.2 copy.23
  116.2 83.4 %reduce-scatter.2.cloned.1.call-done = f32[32,256]{1,0:T(8,128)} async-done(((f32[1024,256]{1,0:T(8,128)}), f32[32,256]{1,0:T(8,128)}) %reduce-scatter.2.cloned.1.call-update) | async-done | bytes 32784 | tf_op jit(solution)/shard_map/reduce_scatter | solution.py:94
  199.5 2.0 fusion.30
  201.5 254.1 %all-reduce.5.cloned.1.call-done = f32[256,256]{1,0:T(8,128)} async-done(((f32[256,256]{1,0:T(8,128)}), f32[256,256]{1,0:T(8,128)}) %all-reduce.5.cloned.1.call-update) | async-done | bytes 262160 | tf_op jit(solution)/shard_map/psum | solution.py:100
  455.6 1.0 broadcast_multiply_fusion.1
  456.7 631.3 %while.33 = (s32[]{:T(128)}, f32[256,256]{1,0:T(8,128)S(1)}, f32[256,256]{0,1:T(8,128)S(1)}, s32[]{:T(128)}, s32[]{:T(128)}) while((s32[]{:T(128)}, f32[256,256]{1,0:T(8,128)S(1)}, f32[256,256]{0,1:T(8,128)S(1)}, s32[]{:T(128)}, s32[]{:T(128)}) %tuple.82), condition=%wide.region_4.5_spmd.clone.clone, body=%wide.region_3.4_spmd.clone.clone.sunk | while | flops 853506 | bytes 801897 | solution.py:23
  1088.0 0.8 copy.25
  1088.8 399.9 %while.34 = (s32[]{:T(128)}, f32[256,256]{1,0:T(8,128)S(1)}, f32[256,256]{1,0:T(8,128)S(1)}, s32[]{:T(128)}, s32[]{:T(128)}, /*index=5*/s32[]{:T(128)}) while((s32[]{:T(128)}, f32[256,256]{1,0:T(8,128)S(1)}, f32[256,256]{1,0:T(8,128)S(1)}, s32[]{:T(128)}, s32[]{:T(128)}, /*index=5*/s32[]{:T(128)}) %tuple.85), condition=%wide.region_6.7_spmd.clone.clone, body=%wide.region_5.6_spmd.clone.clone.sunk | while | flops 787971 | bytes 272501 | solution.py:38
  1089.7 0.6 fusion.55
  1094.4 0.6 fusion.55
  1100.6 0.6 fusion.55
  1106.9 0.6 fusion.55
  1111.6 0.6 fusion.55
  1113.1 0.6 fusion.55
  1117.8 0.6 fusion.55
  1119.4 0.6 fusion.55
  1124.1 0.6 fusion.55
  1130.3 0.6 fusion.55
  1136.6 0.6 fusion.55
  1141.2 0.6 fusion.55
  1142.8 0.6 fusion.55
  1147.5 0.6 fusion.55
  1149.0 0.6 fusion.55
  1153.7 0.6 fusion.55
  1160.0 0.6 fusion.55
  1166.2 0.6 fusion.55
  1170.9 0.6 fusion.55
  1172.5 0.6 fusion.55
  1177.2 0.6 fusion.55
  1178.7 0.6 fusion.55
  1183.4 0.6 fusion.55
  1189.7 0.6 fusion.55
  1195.9 0.6 fusion.55
  1200.6 0.6 fusion.55
  1202.2 0.6 fusion.55
  1206.8 0.6 fusion.55
  1208.4 0.6 fusion.55
  1488.8 1.0 fusion.31
  1489.7 0.7 copy.50
  (3837 shorter events, 808.6 us)
Async XLA Ops:
  7.2 26.2 %copy-start = (f32[1,1,2,256,256]{4,3,2,1,0:T(8,128)S(1)}, f32[1,1,2,256,256]{4,3,2,1,0:T(8,128)}, u32[]{:S(2)}) copy-start(f32[1,1,2,256,256]{4,3,2,1,0:T(8,128)} %param.10) | copy-start | bytes 1572868
  9.1 23.7 %all-to-all-start = ((f32[32,32,256]{2,1,0:T(8,128)}), f32[32,32,256]{2,1,0:T(8,128)S(1)}, u32[]{:S(2)}, u32[]{:S(2)}) async-start(f32[32,32,256]{2,1,0:T(8,128)} %stack.2), calls=%async_computation | async-start | bytes 2097152 | tf_op jit(solution)/shard_map/all_to_all | solution.py:46
  16.7 0.7 copy-start.3
  16.7 94.0 %all-reduce.3.cloned.1.call-start = ((), (), s32[]{:S(2)}) async-start(), calls=%async_computation.2 | async-start | bytes 524288 | tf_op jit(solution)/shard_map/psum | solution.py:74
  34.7 0.7 copy-start.4
  37.9 161.6 %reduce-scatter.2.cloned.1.call-start = ((), (), s32[]{:S(2)}) async-start(), calls=%async_computation.3 | async-start | bytes 1081344 | tf_op jit(solution)/shard_map/reduce_scatter | solution.py:94
  116.1 339.4 %all-reduce.5.cloned.1.call-start = ((), (), s32[]{:S(2)}) async-start(), calls=%async_computation.4 | async-start | bytes 524288 | tf_op jit(solution)/shard_map/psum | solution.py:100
  1088.8 399.9 %copy-start.2 = (f32[32,256]{1,0:T(8,128)S(1)}, f32[32,256]{1,0:T(8,128)}, u32[]{:S(2)}) copy-start(f32[32,256]{1,0:T(8,128)} %reduce-scatter.2.cloned.1.call-done) | copy-start | bytes 98308
  1488.7 1.0 copy-start.1
Sparse Core Ops, SparseCore 0:
  38.0 72.5 all-reduce.2
  116.2 83.2 reduce-scatter.1
  205.6 249.9 all-reduce.4

commit v2 on v0

--- a/solution.py
+++ b/solution.py
@@ -95,7 +95,7 @@
     local_gram = jnp.dot(
         projected.T, projected, precision=lax.Precision.HIGHEST, preferred_element_type=jnp.float32
     )
-    gram_matrix = lax.psum(local_gram, ("row", "col")) / matrix_order
+    gram_matrix = lax.psum(lax.psum(local_gram, "row"), "col") / matrix_order
     lower = cholesky_lower(gram_matrix)
     inverse = lower_inverse(lower)
     factor = lower.T

time: 1530 us -> 1460 us (0.954)
  waiting for transfers between devices: 463 us -> 396 us
    psum x1 -> x2, waiting for transfers between devices: 254 us -> 187 us  [body(): gram_matrix = lax.psum(lax.psum(local_gram, 'row'), 'col') / matrix_order]
  transfers between devices with their start and end apart: 4 -> 5, of which waited for: 4 -> 5; matrix products, arithmetic and copies ran while one was open for 0% -> 0% of each run, Pallas kernels for 0% -> 0%
where the time goes in v2:
time: 1460 us
  local copies, waits for them, and re-layouts  539 us (37%)
  waiting for transfers between devices  396 us (27%)
  loops' own time  206 us (14%)
  other arithmetic  177 us (12%)
  matrix products  126 us (9%)
  between operations  14.6 us (1%)
    another operation x1, loops' own time, cholesky_lower(): return lax.fori_loop(0, size, column_step, jnp.zeros_like(gram))  195 us
    psum x2, waiting for transfers between devices, body(): gram_matrix = lax.psum(lax.psum(local_gram, 'row'), 'col') / matrix_order  187 us
    div x256, other arithmetic, row_step(): (unit - jnp.dot(known, inverse, precision=lax.Precision.HIGHEST)) / pivot  166 us
    dynamic_slice x256, local copies, waits for them, and re-layouts, row_step(): pivot = lax.dynamic_slice_in_dim(row_l, i, 1, 0)[0]  161 us
    dynamic_update_slice x256, local copies, waits for them, and re-layouts, column_step(): return lax.dynamic_update_slice_in_dim(lower, column[:, None], j, 1)  157 us
    dynamic_slice x256, local copies, waits for them, and re-layouts, column_step(): pivot = jnp.sqrt(lax.dynamic_slice_in_dim(column, j, 1, 0)[0])  151 us
    reduce_scatter x1, waiting for transfers between devices, body(): lax.psum_scatter(partial_flat, 'row', scatter_dimension=0, tiled=True)  83.3 us
    psum x1, waiting for transfers between devices, body(): image_block = lax.psum(partial_rows, 'col')  72.3 us
  transfers between devices with their start and end apart: 5, of which 5 were waited for; matrix products, arithmetic and copies ran while one was open for 0% of the time, Pallas kernels for 0%

profile of v2, /device:TPU:2, one launch (start us, length us, event | category | flops | bytes accessed | tf_op | source)
XLA Modules:
  0.0 1459.3 jit_solution(12827107235651050421)
XLA Ops:
  7.2 0.7 all-gather.2.cloned.1.call-update
  8.7 52.4 %all-gather.2.cloned.1.call-done = f32[1024,256]{1,0:T(8,128)} async-done(((f32[32,256]{1,0:T(8,128)}), f32[1024,256]{1,0:T(8,128)}) %all-gather.2.cloned.1.call-update) | async-done | bytes 1048592 | tf_op jit(solution)/shard_map/all_gather | solution.py:45
  61.0 1.8 gather_fusion
  62.8 1.0 convolution_bitcast_fusion.1
  64.8 1.8 fusion.22
  66.6 0.7 copy.30
  67.4 72.3 %all-reduce.4.cloned.1.call-done = f32[256,256]{1,0:T(8,128)} async-done(((f32[256,256]{1,0:T(8,128)}), f32[256,256]{1,0:T(8,128)}) %all-reduce.4.cloned.1.call-update) | async-done | bytes 262160 | tf_op jit(solution)/shard_map/psum | solution.py:72
  139.7 1.1 copy.21
  141.6 2.3 fusion.14
  143.9 1.2 copy.23
  145.2 83.3 %reduce-scatter.2.cloned.1.call-done = f32[32,256]{1,0:T(8,128)} async-done(((f32[1024,256]{1,0:T(8,128)}), f32[32,256]{1,0:T(8,128)}) %reduce-scatter.2.cloned.1.call-update) | async-done | bytes 32784 | tf_op jit(solution)/shard_map/reduce_scatter | solution.py:92
  228.5 1.9 fusion.30
  230.5 112.3 %all-reduce.6.cloned.1.call-done = f32[256,256]{1,0:T(8,128)} async-done(((f32[256,256]{1,0:T(8,128)}), f32[256,256]{1,0:T(8,128)}) %all-reduce.6.cloned.1.call-update) | async-done | bytes 262160 | tf_op jit(solution)/shard_map/psum | solution.py:98
  342.9 75.0 %all-reduce.8.cloned.1.call-done = f32[256,256]{1,0:T(8,128)} async-done(((f32[256,256]{1,0:T(8,128)}), f32[256,256]{1,0:T(8,128)}) %all-reduce.8.cloned.1.call-update) | async-done | bytes 262160 | tf_op jit(solution)/shard_map/psum | solution.py:98
  417.9 1.0 broadcast_multiply_fusion.1
  419.0 631.3 %while.33 = (s32[]{:T(128)}, f32[256,256]{1,0:T(8,128)S(1)}, f32[256,256]{0,1:T(8,128)S(1)}, s32[]{:T(128)}, s32[]{:T(128)}) while((s32[]{:T(128)}, f32[256,256]{1,0:T(8,128)S(1)}, f32[256,256]{0,1:T(8,128)S(1)}, s32[]{:T(128)}, s32[]{:T(128)}) %tuple.82), condition=%wide.region_5.6_spmd.clone.clone, body=%wide.region_4.5_spmd.clone.clone.sunk | while | flops 853506 | bytes 801897 | solution.py:23
  1050.3 0.8 copy.25
  1051.2 399.9 %while.34 = (s32[]{:T(128)}, f32[256,256]{1,0:T(8,128)S(1)}, f32[256,256]{1,0:T(8,128)S(1)}, s32[]{:T(128)}, s32[]{:T(128)}, /*index=5*/s32[]{:T(128)}) while((s32[]{:T(128)}, f32[256,256]{1,0:T(8,128)S(1)}, f32[256,256]{1,0:T(8,128)S(1)}, s32[]{:T(128)}, s32[]{:T(128)}, /*index=5*/s32[]{:T(128)}) %tuple.85), condition=%wide.region_7.8_spmd.clone.clone, body=%wide.region_6.7_spmd.clone.clone.sunk | while | flops 787971 | bytes 272501 | solution.py:38
  1055.1 0.6 fusion.55
  1059.8 0.6 fusion.55
  1061.4 0.6 fusion.55
  1066.1 0.6 fusion.55
  1067.6 0.6 fusion.55
  1072.3 0.6 fusion.55
  1078.6 0.6 fusion.55
  1084.8 0.6 fusion.55
  1089.5 0.6 fusion.55
  1091.1 0.6 fusion.55
  1095.7 0.6 fusion.55
  1097.3 0.6 fusion.55
  1102.0 0.6 fusion.55
  1108.2 0.6 fusion.55
  1114.5 0.6 fusion.55
  1119.2 0.6 fusion.55
  1120.7 0.6 fusion.55
  1125.4 0.6 fusion.55
  1127.0 0.6 fusion.55
  1131.7 0.6 fusion.55
  1137.9 0.6 fusion.55
  1144.2 0.6 fusion.55
  1148.9 0.6 fusion.55
  1150.4 0.6 fusion.55
  1155.1 0.6 fusion.55
  1156.7 0.6 fusion.55
  1161.4 0.6 fusion.55
  1167.6 0.6 fusion.55
  1451.1 1.0 fusion.31
  1452.0 0.7 copy.51
  (3840 shorter events, 808.8 us)
Async XLA Ops:
  7.2 55.7 %copy-start = (f32[1,1,2,256,256]{4,3,2,1,0:T(8,128)S(1)}, f32[1,1,2,256,256]{4,3,2,1,0:T(8,128)}, u32[]{:S(2)}) copy-start(f32[1,1,2,256,256]{4,3,2,1,0:T(8,128)} %param.10) | copy-start | bytes 1572868
  7.2 53.8 %all-gather.2.cloned.1.call-start = ((), (), s32[]{:S(2)}) async-start(), calls=%async_computation.1 | async-start | bytes 1081344 | tf_op jit(solution)/shard_map/all_gather | solution.py:45
  7.9 0.7 copy-start.3
  7.9 131.7 %all-reduce.4.cloned.1.call-start = ((), (), s32[]{:S(2)}) async-start(), calls=%async_computation.2 | async-start | bytes 524288 | tf_op jit(solution)/shard_map/psum | solution.py:72
  64.1 0.7 copy-start.4
  67.4 161.2 %reduce-scatter.2.cloned.1.call-start = ((), (), s32[]{:S(2)}) async-start(), calls=%async_computation.3 | async-start | bytes 1081344 | tf_op jit(solution)/shard_map/reduce_scatter | solution.py:92
  145.1 197.7 %all-reduce.6.cloned.1.call-start = ((), (), s32[]{:S(2)}) async-start(), calls=%async_computation.4 | async-start | bytes 524288 | tf_op jit(solution)/shard_map/psum | solution.py:98
  230.5 187.4 %all-reduce.8.cloned.1.call-start = ((), (), s32[]{:S(2)}) async-start(), calls=%async_computation.5 | async-start | bytes 524288 | tf_op jit(solution)/shard_map/psum | solution.py:98
  1051.1 399.9 %copy-start.2 = (f32[32,256]{1,0:T(8,128)S(1)}, f32[32,256]{1,0:T(8,128)}, u32[]{:S(2)}) copy-start(f32[32,256]{1,0:T(8,128)} %reduce-scatter.2.cloned.1.call-done) | copy-start | bytes 98308
  1451.1 1.0 copy-start.1
Sparse Core Ops, SparseCore 0:
  10.6 50.4 all-gather.1
  67.5 72.1 all-reduce.3
  145.3 83.2 reduce-scatter.1
  232.2 110.6 all-reduce.5
  345.1 72.7 all-reduce.7
